TPU v7x, 512 devices: a whole 4x8x8 slice. The times are simulated.
512 devices in a mesh: sep: 8 (over y), row: 8 (over z), col: 8 (over x, core).
Axes of the slice: x: 4, y: 8, z: 8, core: 2. Of those that a mesh axis runs over, the one named last changes fastest.
Arguments:
- right_sides: float32 [2, 16, 32768], P(None, None, ('sep', 'row', 'col')), may hold values from -6 to 6
- inverse_diag: float32 [8, 4096, 4096], P('sep', ('row', 'col')), may hold values from -0.09375 to 0.09375
- lower_blocks: float32 [8, 2048, 4096], P('sep', ('row', 'col')), may hold values from -0.09375 to 0.09375
- targets: int32 [8, 2048], P('sep', ('row', 'col')), may hold values from 0 to 32767, as said below
- counts: int32 [8, 64], P('sep', ('row', 'col')), may hold values from 0 to 32, as said below
Outputs:
- solution: float32 [2, 16, 32768], P(None, None, ('sep', 'row', 'col'))
Inputs may be any that keep to these rules, and one draw needn't show every extreme that they name: For every separator s and lower row j: targets[s, j] // 4096 > s, except for the last separator whose counts are all zero; and (targets[s, j] % 4096) // 64 == j // 32. The last separator's counts are zero; every other separator has a block with exactly 32 live rows, and the others at least one.
All inputs are finite; a program needn't handle non-finite values.
Results may differ from a plain program's by a relative error of at most 0.0001.
Values sent between devices are 32-bit elements; how exact they have to be, the bound alone decides.
No kernel may reach another device: no remote copies, remote signals or barrier semaphores. Data moves between devices by JAX's collectives and lax.ppermute only.
A program may use at most 64 MiB of HBM per device.

v0:
```python
import jax
import jax.numpy as jnp
from jax import lax
from jax.sharding import PartitionSpec as P

W = 4096


def passed_along(block, axis, distance):
    devices = range(lax.axis_size(axis))
    route = [(i - distance, i) for i in devices if i - distance in devices]
    return lax.ppermute(block, axis, route)


def shards(right_sides, inverse_diag, lower_blocks, targets, counts):
    levels = lax.axis_size("sep")
    own_level = lax.axis_index("sep")
    batches = right_sides.shape[0]
    width_rhs = right_sides.shape[1]
    own_rows = right_sides.shape[2]
    diag_rows = inverse_diag[0]
    lower_rows = lower_blocks[0]
    lower_count = lower_rows.shape[0]
    live = jnp.arange(lower_count, dtype=jnp.int32) < counts[0, 0]
    places = targets[0] // W * own_rows + targets[0] % own_rows

    def solve_piece(segment):
        return lax.dot_general(
            segment,
            diag_rows,
            (((1,), (1,)), ((), ())),
            precision=lax.Precision.HIGHEST,
            preferred_element_type=jnp.float32,
        )

    def lower_piece(segment):
        return lax.dot_general(
            segment,
            lower_rows,
            (((1,), (1,)), ((), ())),
            precision=lax.Precision.HIGHEST,
            preferred_element_type=jnp.float32,
        )

    def one_turn(turn, state):
        carried, solved_all = state
        batch_now = turn // levels
        active = turn % levels == own_level
        batch_now = jnp.clip(batch_now, 0, batches - 1)
        given = lax.dynamic_index_in_dim(right_sides, batch_now, 0, keepdims=False)
        resid = given - lax.dynamic_slice_in_dim(carried, own_level * own_rows, own_rows, 1)
        solved = solve_piece(lax.all_gather(resid, ("row", "col"), axis=1, tiled=True))
        update = lower_piece(lax.all_gather(solved, ("row", "col"), axis=1, tiled=True))
        update = jnp.where(live[None, :], update, jnp.float32(0.0))
        carried = carried.at[:, places].add(update)
        former = lax.dynamic_index_in_dim(solved_all, batch_now, 0, keepdims=False)
        solved_all = lax.dynamic_update_index_in_dim(
            solved_all, jnp.where(active, solved, former), batch_now, 0
        )
        carried = passed_along(carried, "sep", 1)
        return (carried, solved_all)

    turns = batches * levels
    start_carry = jnp.zeros((width_rhs, levels * own_rows), jnp.float32)
    start_solved = jnp.zeros(right_sides.shape, jnp.float32)
    final_carry, solution = lax.fori_loop(0, turns, one_turn, (start_carry, start_solved))
    return solution


def solution(mesh):
    placed = (
        P(None, None, ("sep", "row", "col")),
        P("sep", ("row", "col"), None),
        P("sep", ("row", "col"), None),
        P("sep", ("row", "col")),
        P("sep", ("row", "col")),
    )
    return jax.shard_map(
        shards,
        mesh=mesh,
        in_specs=placed,
        out_specs=P(None, None, ("sep", "row", "col")),
        check_vma=False,
    )
```

profile of v0, /device:TPU:32, one launch (start us, length us, event | category | flops | bytes accessed | tf_op | source)
XLA Modules:
  0.0 1837.8 jit_solution(4809233854240847362)
XLA Ops:
  1.4 1835.8 %while.18 = (s32[]{:T(128)}, f32[16,512]{0,1:T(8,128)S(1)}, f32[2,16,64]{2,1,0:T(8,128)S(1)}, s32[32]{0:T(128)S(1)}, f32[2,16,64]{2,1,0:T(8,128)S(1)}, /*index=5...) while((s32[]{:T(128)}, f32[16,512]{0,1:T(8,128)S(1)}, ...), condition=%wide.region_2.3_spmd.clone, body=%wide.region_0.2_spmd.clone.sunk | while | flops 75500688 | bytes 11338590 | solution.py:66
  1.6 56.5 %all-gather.6 = f32[64,64,16]{1,2,0:T(8,128)S(1)} all-gather(f32[1,64,16]{1,2,0:T(8,128)S(1)} %fusion.22), channel_id=1, replica_groups=mesh['sep'=8,'row'=8,'col'=8] {'row','col'}, dimensions={0}, use_global_device_ids=true | all-gather | bytes 266240 | tf_op jit(solution)/shard_map/while/body/eval_jaxpr/all_gather | solution.py:52
  60.2 49.5 %all-gather.7 = f32[64,64,16]{1,2,0:T(8,128)S(1)} all-gather(f32[1,64,16]{1,2,0:T(8,128)S(1)} %bitcast.71), channel_id=1, replica_groups=mesh['sep'=8,'row'=8,'col'=8] {'row','col'}, dimensions={0}, use_global_device_ids=true | all-gather | bytes 266240 | tf_op jit(solution)/shard_map/while/body/eval_jaxpr/all_gather | solution.py:53
  124.3 48.0 %all-gather.6 = f32[64,64,16]{1,2,0:T(8,128)S(1)} all-gather(f32[1,64,16]{1,2,0:T(8,128)S(1)} %fusion.22), channel_id=1, replica_groups=mesh['sep'=8,'row'=8,'col'=8] {'row','col'}, dimensions={0}, use_global_device_ids=true | all-gather | bytes 266240 | tf_op jit(solution)/shard_map/while/body/eval_jaxpr/all_gather | solution.py:52
  174.4 49.5 %all-gather.7 = f32[64,64,16]{1,2,0:T(8,128)S(1)} all-gather(f32[1,64,16]{1,2,0:T(8,128)S(1)} %bitcast.71), channel_id=1, replica_groups=mesh['sep'=8,'row'=8,'col'=8] {'row','col'}, dimensions={0}, use_global_device_ids=true | all-gather | bytes 266240 | tf_op jit(solution)/shard_map/while/body/eval_jaxpr/all_gather | solution.py:53
  238.5 48.0 %all-gather.6 = f32[64,64,16]{1,2,0:T(8,128)S(1)} all-gather(f32[1,64,16]{1,2,0:T(8,128)S(1)} %fusion.22), channel_id=1, replica_groups=mesh['sep'=8,'row'=8,'col'=8] {'row','col'}, dimensions={0}, use_global_device_ids=true | all-gather | bytes 266240 | tf_op jit(solution)/shard_map/while/body/eval_jaxpr/all_gather | solution.py:52
  288.6 49.5 %all-gather.7 = f32[64,64,16]{1,2,0:T(8,128)S(1)} all-gather(f32[1,64,16]{1,2,0:T(8,128)S(1)} %bitcast.71), channel_id=1, replica_groups=mesh['sep'=8,'row'=8,'col'=8] {'row','col'}, dimensions={0}, use_global_device_ids=true | all-gather | bytes 266240 | tf_op jit(solution)/shard_map/while/body/eval_jaxpr/all_gather | solution.py:53
  402.8 49.5 %all-gather.7 = f32[64,64,16]{1,2,0:T(8,128)S(1)} all-gather(f32[1,64,16]{1,2,0:T(8,128)S(1)} %bitcast.71), channel_id=1, replica_groups=mesh['sep'=8,'row'=8,'col'=8] {'row','col'}, dimensions={0}, use_global_device_ids=true | all-gather | bytes 266240 | tf_op jit(solution)/shard_map/while/body/eval_jaxpr/all_gather | solution.py:53
  517.0 49.5 %all-gather.7 = f32[64,64,16]{1,2,0:T(8,128)S(1)} all-gather(f32[1,64,16]{1,2,0:T(8,128)S(1)} %bitcast.71), channel_id=1, replica_groups=mesh['sep'=8,'row'=8,'col'=8] {'row','col'}, dimensions={0}, use_global_device_ids=true | all-gather | bytes 266240 | tf_op jit(solution)/shard_map/while/body/eval_jaxpr/all_gather | solution.py:53
  631.3 49.5 %all-gather.7 = f32[64,64,16]{1,2,0:T(8,128)S(1)} all-gather(f32[1,64,16]{1,2,0:T(8,128)S(1)} %bitcast.71), channel_id=1, replica_groups=mesh['sep'=8,'row'=8,'col'=8] {'row','col'}, dimensions={0}, use_global_device_ids=true | all-gather | bytes 266240 | tf_op jit(solution)/shard_map/while/body/eval_jaxpr/all_gather | solution.py:53
  745.5 49.5 %all-gather.7 = f32[64,64,16]{1,2,0:T(8,128)S(1)} all-gather(f32[1,64,16]{1,2,0:T(8,128)S(1)} %bitcast.71), channel_id=1, replica_groups=mesh['sep'=8,'row'=8,'col'=8] {'row','col'}, dimensions={0}, use_global_device_ids=true | all-gather | bytes 266240 | tf_op jit(solution)/shard_map/while/body/eval_jaxpr/all_gather | solution.py:53
  859.7 49.5 %all-gather.7 = f32[64,64,16]{1,2,0:T(8,128)S(1)} all-gather(f32[1,64,16]{1,2,0:T(8,128)S(1)} %bitcast.71), channel_id=1, replica_groups=mesh['sep'=8,'row'=8,'col'=8] {'row','col'}, dimensions={0}, use_global_device_ids=true | all-gather | bytes 266240 | tf_op jit(solution)/shard_map/while/body/eval_jaxpr/all_gather | solution.py:53
  973.9 49.5 %all-gather.7 = f32[64,64,16]{1,2,0:T(8,128)S(1)} all-gather(f32[1,64,16]{1,2,0:T(8,128)S(1)} %bitcast.71), channel_id=1, replica_groups=mesh['sep'=8,'row'=8,'col'=8] {'row','col'}, dimensions={0}, use_global_device_ids=true | all-gather | bytes 266240 | tf_op jit(solution)/shard_map/while/body/eval_jaxpr/all_gather | solution.py:53
  1088.1 49.5 %all-gather.7 = f32[64,64,16]{1,2,0:T(8,128)S(1)} all-gather(f32[1,64,16]{1,2,0:T(8,128)S(1)} %bitcast.71), channel_id=1, replica_groups=mesh['sep'=8,'row'=8,'col'=8] {'row','col'}, dimensions={0}, use_global_device_ids=true | all-gather | bytes 266240 | tf_op jit(solution)/shard_map/while/body/eval_jaxpr/all_gather | solution.py:53
  1152.2 48.0 %all-gather.6 = f32[64,64,16]{1,2,0:T(8,128)S(1)} all-gather(f32[1,64,16]{1,2,0:T(8,128)S(1)} %fusion.22), channel_id=1, replica_groups=mesh['sep'=8,'row'=8,'col'=8] {'row','col'}, dimensions={0}, use_global_device_ids=true | all-gather | bytes 266240 | tf_op jit(solution)/shard_map/while/body/eval_jaxpr/all_gather | solution.py:52
  1202.3 49.5 %all-gather.7 = f32[64,64,16]{1,2,0:T(8,128)S(1)} all-gather(f32[1,64,16]{1,2,0:T(8,128)S(1)} %bitcast.71), channel_id=1, replica_groups=mesh['sep'=8,'row'=8,'col'=8] {'row','col'}, dimensions={0}, use_global_device_ids=true | all-gather | bytes 266240 | tf_op jit(solution)/shard_map/while/body/eval_jaxpr/all_gather | solution.py:53
  1266.4 48.0 %all-gather.6 = f32[64,64,16]{1,2,0:T(8,128)S(1)} all-gather(f32[1,64,16]{1,2,0:T(8,128)S(1)} %fusion.22), channel_id=1, replica_groups=mesh['sep'=8,'row'=8,'col'=8] {'row','col'}, dimensions={0}, use_global_device_ids=true | all-gather | bytes 266240 | tf_op jit(solution)/shard_map/while/body/eval_jaxpr/all_gather | solution.py:52
  1316.5 49.5 %all-gather.7 = f32[64,64,16]{1,2,0:T(8,128)S(1)} all-gather(f32[1,64,16]{1,2,0:T(8,128)S(1)} %bitcast.71), channel_id=1, replica_groups=mesh['sep'=8,'row'=8,'col'=8] {'row','col'}, dimensions={0}, use_global_device_ids=true | all-gather | bytes 266240 | tf_op jit(solution)/shard_map/while/body/eval_jaxpr/all_gather | solution.py:53
  1380.6 48.0 %all-gather.6 = f32[64,64,16]{1,2,0:T(8,128)S(1)} all-gather(f32[1,64,16]{1,2,0:T(8,128)S(1)} %fusion.22), channel_id=1, replica_groups=mesh['sep'=8,'row'=8,'col'=8] {'row','col'}, dimensions={0}, use_global_device_ids=true | all-gather | bytes 266240 | tf_op jit(solution)/shard_map/while/body/eval_jaxpr/all_gather | solution.py:52
  1430.7 49.5 %all-gather.7 = f32[64,64,16]{1,2,0:T(8,128)S(1)} all-gather(f32[1,64,16]{1,2,0:T(8,128)S(1)} %bitcast.71), channel_id=1, replica_groups=mesh['sep'=8,'row'=8,'col'=8] {'row','col'}, dimensions={0}, use_global_device_ids=true | all-gather | bytes 266240 | tf_op jit(solution)/shard_map/while/body/eval_jaxpr/all_gather | solution.py:53
  1544.9 49.5 %all-gather.7 = f32[64,64,16]{1,2,0:T(8,128)S(1)} all-gather(f32[1,64,16]{1,2,0:T(8,128)S(1)} %bitcast.71), channel_id=1, replica_groups=mesh['sep'=8,'row'=8,'col'=8] {'row','col'}, dimensions={0}, use_global_device_ids=true | all-gather | bytes 266240 | tf_op jit(solution)/shard_map/while/body/eval_jaxpr/all_gather | solution.py:53
  1609.0 48.0 %all-gather.6 = f32[64,64,16]{1,2,0:T(8,128)S(1)} all-gather(f32[1,64,16]{1,2,0:T(8,128)S(1)} %fusion.22), channel_id=1, replica_groups=mesh['sep'=8,'row'=8,'col'=8] {'row','col'}, dimensions={0}, use_global_device_ids=true | all-gather | bytes 266240 | tf_op jit(solution)/shard_map/while/body/eval_jaxpr/all_gather | solution.py:52
  1659.1 49.5 %all-gather.7 = f32[64,64,16]{1,2,0:T(8,128)S(1)} all-gather(f32[1,64,16]{1,2,0:T(8,128)S(1)} %bitcast.71), channel_id=1, replica_groups=mesh['sep'=8,'row'=8,'col'=8] {'row','col'}, dimensions={0}, use_global_device_ids=true | all-gather | bytes 266240 | tf_op jit(solution)/shard_map/while/body/eval_jaxpr/all_gather | solution.py:53
  1773.3 49.5 %all-gather.7 = f32[64,64,16]{1,2,0:T(8,128)S(1)} all-gather(f32[1,64,16]{1,2,0:T(8,128)S(1)} %bitcast.71), channel_id=1, replica_groups=mesh['sep'=8,'row'=8,'col'=8] {'row','col'}, dimensions={0}, use_global_device_ids=true | all-gather | bytes 266240 | tf_op jit(solution)/shard_map/while/body/eval_jaxpr/all_gather | solution.py:53
  (338 shorter events, 699.8 us)
Async XLA Ops:
  58.1 1.2 copy-start
  112.5 11.7 collective-permute-start
  226.7 11.7 collective-permute-start
  286.5 1.2 copy-start
  340.9 11.7 collective-permute-start
  400.7 1.2 copy-start
  455.1 11.7 collective-permute-start
  514.9 1.2 copy-start
  569.3 11.7 collective-permute-start
  629.1 1.2 copy-start
  683.5 11.7 collective-permute-start
  797.7 11.7 collective-permute-start
  857.5 1.2 copy-start
  911.9 11.7 collective-permute-start
  971.7 1.2 copy-start
  1026.1 11.7 collective-permute-start
  1085.9 1.2 copy-start
  1140.3 11.7 collective-permute-start
  1254.5 11.7 collective-permute-start
  1368.7 11.7 collective-permute-start
  1482.9 11.7 collective-permute-start
  1597.1 11.7 collective-permute-start
  1711.3 11.7 collective-permute-start
  1825.5 11.7 collective-permute-start
  (27 other events, 28.5 us)
where the time goes:
time: 1840 us
  blocking collectives  1570 us (85%)
  waiting for transfers between devices  155 us (8%)
  local copies, waits for them, and re-layouts  33.2 us (2%)
  starting transfers between devices  31.4 us (2%)
  other arithmetic  25.5 us (1%)
  matrix products  23 us (1%)
    all_gather x16, blocking collectives, one_turn(): lax.all_gather(solved, ('row', 'col'), axis=1, tiled=True)  792 us
    all_gather x16, blocking collectives, one_turn(): lax.all_gather(resid, ('row', 'col'), axis=1, tiled=True)  776 us
    ppermute x16, waiting for transfers between devices, passed_along(): return lax.ppermute(block, axis, route)  155 us
  transfers between devices with their start and end apart: 16, of which 16 were waited for; matrix products, arithmetic and copies ran while one was open for 0% of the time, Pallas kernels for 0%

commit v1 on v0

--- a/solution.py
+++ b/solution.py
@@ -4,6 +4,11 @@
 from jax.sharding import PartitionSpec as P
 
 W = 4096
+
+
+def _rest_case(x0):
+    row_out = jnp.concatenate(lax.axis_size(("row", "col")) * [x0], axis=1)
+    return lax.all_to_all(row_out, ("row", "col"), split_axis=1, concat_axis=1, tiled=True)
 
 
 def passed_along(block, axis, distance):
@@ -49,7 +54,7 @@
         batch_now = jnp.clip(batch_now, 0, batches - 1)
         given = lax.dynamic_index_in_dim(right_sides, batch_now, 0, keepdims=False)
         resid = given - lax.dynamic_slice_in_dim(carried, own_level * own_rows, own_rows, 1)
-        solved = solve_piece(lax.all_gather(resid, ("row", "col"), axis=1, tiled=True))
+        solved = solve_piece(_rest_case(resid))
         update = lower_piece(lax.all_gather(solved, ("row", "col"), axis=1, tiled=True))
         update = jnp.where(live[None, :], update, jnp.float32(0.0))
         carried = carried.at[:, places].add(update)

time: 1840 us -> 1430 us (0.78)
  blocking collectives: 1570 us -> 783 us
  waiting for transfers between devices: 155 us -> 350 us
  starting transfers between devices: 31.4 us -> 137 us
  local copies, waits for them, and re-layouts: 33.2 us -> 81.8 us
  other arithmetic: 25.5 us -> 45.2 us
    all_gather x16 -> x0, blocking collectives: 776 us -> none  [one_turn(): lax.all_gather(resid, ('row', 'col'), axis=1, tiled=True)]
    all_to_all x0 -> x16, waiting for transfers between devices: none -> 195 us  [_rest_case(): lax.all_to_all(row_out, ('row', 'col'), split_axis=1, concat_axis=1, tile...]
    all_to_all x0 -> x16, starting transfers between devices: none -> 105 us  [_rest_case(): lax.all_to_all(row_out, ('row', 'col'), split_axis=1, concat_axis=1, tile...]
    while x128 -> x144, local copies, waits for them, and re-layouts: 24.4 us -> 50.5 us
    all_to_all x0 -> x80, local copies, waits for them, and re-layouts: none -> 22.4 us  [_rest_case(): lax.all_to_all(row_out, ('row', 'col'), split_axis=1, concat_axis=1, tile...]
    all_to_all x0 -> x16, other arithmetic: none -> 19.7 us  [_rest_case(): lax.all_to_all(row_out, ('row', 'col'), split_axis=1, concat_axis=1, tile...]
  transfers between devices with their start and end apart: 16 -> 32, of which waited for: 16 -> 32; matrix products, arithmetic and copies ran while one was open for 0% -> 1% of each run, Pallas kernels for 0% -> 0%
where the time goes in v1:
time: 1430 us; the launch traced here: 1420 us
  blocking collectives  783 us (55%)
  waiting for transfers between devices  350 us (24%)
  starting transfers between devices  137 us (10%)
  local copies, waits for them, and re-layouts  81.8 us (6%)
  other arithmetic  45.2 us (3%)
  matrix products  23 us (2%)
    all_gather x16, blocking collectives, one_turn(): lax.all_gather(solved, ('row', 'col'), axis=1, tiled=True)  783 us
    all_to_all x16, waiting for transfers between devices, _rest_case(): lax.all_to_all(row_out, ('row', 'col'), split_axis=1, concat_axis=1, tile...  195 us
    ppermute x16, waiting for transfers between devices, passed_along(): return lax.ppermute(block, axis, route)  155 us
    all_to_all x16, starting transfers between devices, _rest_case(): lax.all_to_all(row_out, ('row', 'col'), split_axis=1, concat_axis=1, tile...  105 us
    while x144, local copies, waits for them, and re-layouts  50.5 us
    ppermute x16, starting transfers between devices, passed_along(): return lax.ppermute(block, axis, route)  31.4 us
  transfers between devices with their start and end apart: 32, of which 32 were waited for; matrix products, arithmetic and copies ran while one was open for 1% of the time, Pallas kernels for 0%

profile of v1, /device:TPU:32, one launch (start us, length us, event | category | flops | bytes accessed | tf_op | source)
XLA Modules:
  0.0 1422.3 jit_solution(3346094493391141695)
XLA Ops:
  1.4 1420.2 %while.18 = (s32[]{:T(128)}, f32[16,512]{0,1:T(8,128)S(1)}, f32[2,16,64]{2,1,0:T(8,128)S(1)}, s32[32]{0:T(128)S(1)}, f32[2,16,64]{2,1,0:T(8,128)S(1)}, /*index=5...) while((s32[]{:T(128)}, f32[16,512]{0,1:T(8,128)S(1)}, ...), condition=%wide.region_2.3_spmd.clone, body=%wide.region_0.2_spmd.clone.sunk | while | flops 75500688 | bytes 15004562 | solution.py:71
  3.3 13.8 all-to-all-start
  17.8 12.2 all-to-all-done
  34.0 48.9 %all-gather.3 = f32[64,64,16]{1,2,0:T(8,128)S(1)} all-gather(f32[1,64,16]{1,2,0:T(8,128)S(1)} %bitcast.71), channel_id=1, replica_groups=mesh['sep'=8,'row'=8,'col'=8] {'row','col'}, dimensions={0}, use_global_device_ids=true | all-gather | bytes 266240 | tf_op jit(solution)/shard_map/while/body/eval_jaxpr/all_gather | solution.py:58
  106.1 12.2 all-to-all-done
  122.3 48.9 %all-gather.3 = f32[64,64,16]{1,2,0:T(8,128)S(1)} all-gather(f32[1,64,16]{1,2,0:T(8,128)S(1)} %bitcast.71), channel_id=1, replica_groups=mesh['sep'=8,'row'=8,'col'=8] {'row','col'}, dimensions={0}, use_global_device_ids=true | all-gather | bytes 266240 | tf_op jit(solution)/shard_map/while/body/eval_jaxpr/all_gather | solution.py:58
  194.4 12.2 all-to-all-done
  210.6 48.9 %all-gather.3 = f32[64,64,16]{1,2,0:T(8,128)S(1)} all-gather(f32[1,64,16]{1,2,0:T(8,128)S(1)} %bitcast.71), channel_id=1, replica_groups=mesh['sep'=8,'row'=8,'col'=8] {'row','col'}, dimensions={0}, use_global_device_ids=true | all-gather | bytes 266240 | tf_op jit(solution)/shard_map/while/body/eval_jaxpr/all_gather | solution.py:58
  298.9 48.9 %all-gather.3 = f32[64,64,16]{1,2,0:T(8,128)S(1)} all-gather(f32[1,64,16]{1,2,0:T(8,128)S(1)} %bitcast.71), channel_id=1, replica_groups=mesh['sep'=8,'row'=8,'col'=8] {'row','col'}, dimensions={0}, use_global_device_ids=true | all-gather | bytes 266240 | tf_op jit(solution)/shard_map/while/body/eval_jaxpr/all_gather | solution.py:58
  387.2 48.9 %all-gather.3 = f32[64,64,16]{1,2,0:T(8,128)S(1)} all-gather(f32[1,64,16]{1,2,0:T(8,128)S(1)} %bitcast.71), channel_id=1, replica_groups=mesh['sep'=8,'row'=8,'col'=8] {'row','col'}, dimensions={0}, use_global_device_ids=true | all-gather | bytes 266240 | tf_op jit(solution)/shard_map/while/body/eval_jaxpr/all_gather | solution.py:58
  475.5 48.9 %all-gather.3 = f32[64,64,16]{1,2,0:T(8,128)S(1)} all-gather(f32[1,64,16]{1,2,0:T(8,128)S(1)} %bitcast.71), channel_id=1, replica_groups=mesh['sep'=8,'row'=8,'col'=8] {'row','col'}, dimensions={0}, use_global_device_ids=true | all-gather | bytes 266240 | tf_op jit(solution)/shard_map/while/body/eval_jaxpr/all_gather | solution.py:58
  563.8 48.9 %all-gather.3 = f32[64,64,16]{1,2,0:T(8,128)S(1)} all-gather(f32[1,64,16]{1,2,0:T(8,128)S(1)} %bitcast.71), channel_id=1, replica_groups=mesh['sep'=8,'row'=8,'col'=8] {'row','col'}, dimensions={0}, use_global_device_ids=true | all-gather | bytes 266240 | tf_op jit(solution)/shard_map/while/body/eval_jaxpr/all_gather | solution.py:58
  635.8 12.2 all-to-all-done
  652.0 48.9 %all-gather.3 = f32[64,64,16]{1,2,0:T(8,128)S(1)} all-gather(f32[1,64,16]{1,2,0:T(8,128)S(1)} %bitcast.71), channel_id=1, replica_groups=mesh['sep'=8,'row'=8,'col'=8] {'row','col'}, dimensions={0}, use_global_device_ids=true | all-gather | bytes 266240 | tf_op jit(solution)/shard_map/while/body/eval_jaxpr/all_gather | solution.py:58
  740.3 48.9 %all-gather.3 = f32[64,64,16]{1,2,0:T(8,128)S(1)} all-gather(f32[1,64,16]{1,2,0:T(8,128)S(1)} %bitcast.71), channel_id=1, replica_groups=mesh['sep'=8,'row'=8,'col'=8] {'row','col'}, dimensions={0}, use_global_device_ids=true | all-gather | bytes 266240 | tf_op jit(solution)/shard_map/while/body/eval_jaxpr/all_gather | solution.py:58
  828.6 48.9 %all-gather.3 = f32[64,64,16]{1,2,0:T(8,128)S(1)} all-gather(f32[1,64,16]{1,2,0:T(8,128)S(1)} %bitcast.71), channel_id=1, replica_groups=mesh['sep'=8,'row'=8,'col'=8] {'row','col'}, dimensions={0}, use_global_device_ids=true | all-gather | bytes 266240 | tf_op jit(solution)/shard_map/while/body/eval_jaxpr/all_gather | solution.py:58
  916.9 48.9 %all-gather.3 = f32[64,64,16]{1,2,0:T(8,128)S(1)} all-gather(f32[1,64,16]{1,2,0:T(8,128)S(1)} %bitcast.71), channel_id=1, replica_groups=mesh['sep'=8,'row'=8,'col'=8] {'row','col'}, dimensions={0}, use_global_device_ids=true | all-gather | bytes 266240 | tf_op jit(solution)/shard_map/while/body/eval_jaxpr/all_gather | solution.py:58
  989.0 12.2 all-to-all-done
  1005.2 48.9 %all-gather.3 = f32[64,64,16]{1,2,0:T(8,128)S(1)} all-gather(f32[1,64,16]{1,2,0:T(8,128)S(1)} %bitcast.71), channel_id=1, replica_groups=mesh['sep'=8,'row'=8,'col'=8] {'row','col'}, dimensions={0}, use_global_device_ids=true | all-gather | bytes 266240 | tf_op jit(solution)/shard_map/while/body/eval_jaxpr/all_gather | solution.py:58
  1077.2 12.2 all-to-all-done
  1093.5 48.9 %all-gather.3 = f32[64,64,16]{1,2,0:T(8,128)S(1)} all-gather(f32[1,64,16]{1,2,0:T(8,128)S(1)} %bitcast.71), channel_id=1, replica_groups=mesh['sep'=8,'row'=8,'col'=8] {'row','col'}, dimensions={0}, use_global_device_ids=true | all-gather | bytes 266240 | tf_op jit(solution)/shard_map/while/body/eval_jaxpr/all_gather | solution.py:58
  1181.8 48.9 %all-gather.3 = f32[64,64,16]{1,2,0:T(8,128)S(1)} all-gather(f32[1,64,16]{1,2,0:T(8,128)S(1)} %bitcast.71), channel_id=1, replica_groups=mesh['sep'=8,'row'=8,'col'=8] {'row','col'}, dimensions={0}, use_global_device_ids=true | all-gather | bytes 266240 | tf_op jit(solution)/shard_map/while/body/eval_jaxpr/all_gather | solution.py:58
  1270.1 48.9 %all-gather.3 = f32[64,64,16]{1,2,0:T(8,128)S(1)} all-gather(f32[1,64,16]{1,2,0:T(8,128)S(1)} %bitcast.71), channel_id=1, replica_groups=mesh['sep'=8,'row'=8,'col'=8] {'row','col'}, dimensions={0}, use_global_device_ids=true | all-gather | bytes 266240 | tf_op jit(solution)/shard_map/while/body/eval_jaxpr/all_gather | solution.py:58
  1358.3 48.9 %all-gather.3 = f32[64,64,16]{1,2,0:T(8,128)S(1)} all-gather(f32[1,64,16]{1,2,0:T(8,128)S(1)} %bitcast.71), channel_id=1, replica_groups=mesh['sep'=8,'row'=8,'col'=8] {'row','col'}, dimensions={0}, use_global_device_ids=true | all-gather | bytes 266240 | tf_op jit(solution)/shard_map/while/body/eval_jaxpr/all_gather | solution.py:58
  (466 shorter events, 550.0 us)
Async XLA Ops:
  3.3 26.7 %all-to-all-start = ((f32[64,1,1024]{2,1,0:T(1,128)}), f32[64,1,1024]{2,1,0:T(1,128)S(1)}, u32[]{:S(2)}, u32[]{:S(2)}) async-start(f32[64,1,1024]{2,1,0:T(1,128)} %reshape.58), calls=%async_computation | async-start | bytes 524288 | tf_op jit(solution)/shard_map/while/body/eval_jaxpr/all_to_all | solution.py:11
  85.7 11.7 collective-permute-start
  99.3 19.0 %all-to-all-start = ((f32[64,1,1024]{2,1,0:T(1,128)}), f32[64,1,1024]{2,1,0:T(1,128)S(1)}, u32[]{:S(2)}, u32[]{:S(2)}) async-start(f32[64,1,1024]{2,1,0:T(1,128)} %reshape.58), calls=%async_computation | async-start | bytes 524288 | tf_op jit(solution)/shard_map/while/body/eval_jaxpr/all_to_all | solution.py:11
  187.6 19.0 %all-to-all-start = ((f32[64,1,1024]{2,1,0:T(1,128)}), f32[64,1,1024]{2,1,0:T(1,128)S(1)}, u32[]{:S(2)}, u32[]{:S(2)}) async-start(f32[64,1,1024]{2,1,0:T(1,128)} %reshape.58), calls=%async_computation | async-start | bytes 524288 | tf_op jit(solution)/shard_map/while/body/eval_jaxpr/all_to_all | solution.py:11
  262.2 11.7 collective-permute-start
  275.9 19.0 %all-to-all-start = ((f32[64,1,1024]{2,1,0:T(1,128)}), f32[64,1,1024]{2,1,0:T(1,128)S(1)}, u32[]{:S(2)}, u32[]{:S(2)}) async-start(f32[64,1,1024]{2,1,0:T(1,128)} %reshape.58), calls=%async_computation | async-start | bytes 524288 | tf_op jit(solution)/shard_map/while/body/eval_jaxpr/all_to_all | solution.py:11
  350.5 11.7 collective-permute-start
  364.1 19.0 %all-to-all-start = ((f32[64,1,1024]{2,1,0:T(1,128)}), f32[64,1,1024]{2,1,0:T(1,128)S(1)}, u32[]{:S(2)}, u32[]{:S(2)}) async-start(f32[64,1,1024]{2,1,0:T(1,128)} %reshape.58), calls=%async_computation | async-start | bytes 524288 | tf_op jit(solution)/shard_map/while/body/eval_jaxpr/all_to_all | solution.py:11
  452.4 19.0 %all-to-all-start = ((f32[64,1,1024]{2,1,0:T(1,128)}), f32[64,1,1024]{2,1,0:T(1,128)S(1)}, u32[]{:S(2)}, u32[]{:S(2)}) async-start(f32[64,1,1024]{2,1,0:T(1,128)} %reshape.58), calls=%async_computation | async-start | bytes 524288 | tf_op jit(solution)/shard_map/while/body/eval_jaxpr/all_to_all | solution.py:11
  540.7 19.0 %all-to-all-start = ((f32[64,1,1024]{2,1,0:T(1,128)}), f32[64,1,1024]{2,1,0:T(1,128)S(1)}, u32[]{:S(2)}, u32[]{:S(2)}) async-start(f32[64,1,1024]{2,1,0:T(1,128)} %reshape.58), calls=%async_computation | async-start | bytes 524288 | tf_op jit(solution)/shard_map/while/body/eval_jaxpr/all_to_all | solution.py:11
  629.0 19.0 %all-to-all-start = ((f32[64,1,1024]{2,1,0:T(1,128)}), f32[64,1,1024]{2,1,0:T(1,128)S(1)}, u32[]{:S(2)}, u32[]{:S(2)}) async-start(f32[64,1,1024]{2,1,0:T(1,128)} %reshape.58), calls=%async_computation | async-start | bytes 524288 | tf_op jit(solution)/shard_map/while/body/eval_jaxpr/all_to_all | solution.py:11
  703.7 11.7 collective-permute-start
  717.3 19.0 %all-to-all-start = ((f32[64,1,1024]{2,1,0:T(1,128)}), f32[64,1,1024]{2,1,0:T(1,128)S(1)}, u32[]{:S(2)}, u32[]{:S(2)}) async-start(f32[64,1,1024]{2,1,0:T(1,128)} %reshape.58), calls=%async_computation | async-start | bytes 524288 | tf_op jit(solution)/shard_map/while/body/eval_jaxpr/all_to_all | solution.py:11
  792.0 11.7 collective-permute-start
  805.6 19.0 %all-to-all-start = ((f32[64,1,1024]{2,1,0:T(1,128)}), f32[64,1,1024]{2,1,0:T(1,128)S(1)}, u32[]{:S(2)}, u32[]{:S(2)}) async-start(f32[64,1,1024]{2,1,0:T(1,128)} %reshape.58), calls=%async_computation | async-start | bytes 524288 | tf_op jit(solution)/shard_map/while/body/eval_jaxpr/all_to_all | solution.py:11
  893.9 19.0 %all-to-all-start = ((f32[64,1,1024]{2,1,0:T(1,128)}), f32[64,1,1024]{2,1,0:T(1,128)S(1)}, u32[]{:S(2)}, u32[]{:S(2)}) async-start(f32[64,1,1024]{2,1,0:T(1,128)} %reshape.58), calls=%async_computation | async-start | bytes 524288 | tf_op jit(solution)/shard_map/while/body/eval_jaxpr/all_to_all | solution.py:11
  982.1 19.0 %all-to-all-start = ((f32[64,1,1024]{2,1,0:T(1,128)}), f32[64,1,1024]{2,1,0:T(1,128)S(1)}, u32[]{:S(2)}, u32[]{:S(2)}) async-start(f32[64,1,1024]{2,1,0:T(1,128)} %reshape.58), calls=%async_computation | async-start | bytes 524288 | tf_op jit(solution)/shard_map/while/body/eval_jaxpr/all_to_all | solution.py:11
  1056.8 11.7 collective-permute-start
  1070.4 19.0 %all-to-all-start = ((f32[64,1,1024]{2,1,0:T(1,128)}), f32[64,1,1024]{2,1,0:T(1,128)S(1)}, u32[]{:S(2)}, u32[]{:S(2)}) async-start(f32[64,1,1024]{2,1,0:T(1,128)} %reshape.58), calls=%async_computation | async-start | bytes 524288 | tf_op jit(solution)/shard_map/while/body/eval_jaxpr/all_to_all | solution.py:11
  1145.1 11.7 collective-permute-start
  1158.7 19.0 %all-to-all-start = ((f32[64,1,1024]{2,1,0:T(1,128)}), f32[64,1,1024]{2,1,0:T(1,128)S(1)}, u32[]{:S(2)}, u32[]{:S(2)}) async-start(f32[64,1,1024]{2,1,0:T(1,128)} %reshape.58), calls=%async_computation | async-start | bytes 524288 | tf_op jit(solution)/shard_map/while/body/eval_jaxpr/all_to_all | solution.py:11
  1233.4 11.7 collective-permute-start
  1247.0 19.0 %all-to-all-start = ((f32[64,1,1024]{2,1,0:T(1,128)}), f32[64,1,1024]{2,1,0:T(1,128)S(1)}, u32[]{:S(2)}, u32[]{:S(2)}) async-start(f32[64,1,1024]{2,1,0:T(1,128)} %reshape.58), calls=%async_computation | async-start | bytes 524288 | tf_op jit(solution)/shard_map/while/body/eval_jaxpr/all_to_all | solution.py:11
  1335.3 19.0 %all-to-all-start = ((f32[64,1,1024]{2,1,0:T(1,128)}), f32[64,1,1024]{2,1,0:T(1,128)S(1)}, u32[]{:S(2)}, u32[]{:S(2)}) async-start(f32[64,1,1024]{2,1,0:T(1,128)} %reshape.58), calls=%async_computation | async-start | bytes 524288 | tf_op jit(solution)/shard_map/while/body/eval_jaxpr/all_to_all | solution.py:11
  (43 other events, 131.7 us)
